TPU v7x, 128 devices: a whole 4x4x4 slice. The times are simulated.
128 devices in a mesh: ang: 64 (over x, y_lo, z, core), pix: 2 (over y_hi).
Axes of the slice: x: 4, y: 4 (y_hi: 2, y_lo: 2; y = y_hi * 2 + y_lo), z: 4, core: 2. Of those that a mesh axis runs over, the one named last changes fastest.
Arguments:
- grads: bfloat16 [2, 4096, 128, 512], P(None, 'ang', 'pix')
- circle_pos: int32 [4096], replicated, may hold values from 0 to 4095, as said below
- harmonics: int32 [256], replicated, may hold values from 0 to 4095, as said below
- support: int32 [128, 512], replicated, may hold values 0 or 1
Outputs:
- update: bfloat16 [2, 4096, 128, 512], P(None, 'ang', 'pix')
- harmonic_rms: float32 [256], replicated
Inputs may be any that keep to these rules, and one draw needn't show every extreme that they name: `circle_pos`: the stored angles form 64 aligned blocks of 64 rows; block b holds the circle positions r_b + 64 * j for j = 0 to 63 in this order, and the 64 values r_b are distinct. `harmonics`: 256 distinct harmonic numbers, among them 0 and 4095.
All inputs are finite; a program needn't handle non-finite values.
Results may differ from a plain program's by a relative error of at most 0.015.
Values may be sent and summed in bfloat16 or wider, within the bound.
No kernel may reach another device: no remote copies, remote signals or barrier semaphores. Data moves between devices by JAX's collectives and lax.ppermute only.
A program may use at most 192 MiB of HBM per device.

v0:
```python
import math
import jax
import jax.numpy as jnp
from jax import lax
from jax.sharding import PartitionSpec as P


def phase_pair(product, modulus):
    radians = (product % modulus).astype(jnp.float32) * (2.0 * math.pi / modulus)
    return (jnp.cos(radians), jnp.sin(radians))


def split_parts(value):
    if value.dtype == jnp.bfloat16:
        return (value,)
    high = value.astype(jnp.bfloat16)
    low = (value - high.astype(jnp.float32)).astype(jnp.bfloat16)
    return (high, low)


def split_einsum(form, left, right):
    left_parts = split_parts(left)
    right_parts = split_parts(right)
    total = None
    for left_rank, left_piece in enumerate(left_parts):
        for right_rank, right_piece in enumerate(right_parts):
            if left_rank + right_rank <= 1:
                term = jnp.einsum(form, left_piece, right_piece, preferred_element_type=jnp.float32)
                total = term if total is None else total + term
    return total


def normalize(coef_re, coef_im, weight, cell_count):
    square_sums = jnp.sum(weight[None, :] * (coef_re * coef_re + coef_im * coef_im), axis=1)
    totals = lax.psum(square_sums, ("ang", "pix"))
    harmonic_rms = jnp.sqrt(totals / cell_count + 1e-06)
    factor = weight[None, :] / harmonic_rms[:, None]
    return (coef_re * factor, coef_im * factor, harmonic_rms)


def direct_path(grads, circle_pos, harmonics, weight, cell_count):
    angle_count = circle_pos.shape[0]
    kept_count = harmonics.shape[0]
    moved = lax.all_to_all(grads, "ang", split_axis=2, concat_axis=1, tiled=True)
    row_local = moved.shape[2]
    col_count = moved.shape[3]
    flat = moved.reshape(2, angle_count, row_local * col_count)
    pixel_count = flat.shape[2]
    phase_cos, phase_sin = phase_pair(harmonics[:, None] * circle_pos[None, :], angle_count)
    table = jnp.concatenate((phase_cos, phase_sin), 0)
    products = split_einsum("ka,ap->kp", table, jnp.concatenate((flat[0], flat[1]), 1))
    scale = 1.0 / math.sqrt(angle_count)
    coef_re = (products[:kept_count, :pixel_count] + products[kept_count:, pixel_count:]) * scale
    coef_im = (products[:kept_count, pixel_count:] - products[kept_count:, :pixel_count]) * scale
    step_re, step_im, harmonic_rms = normalize(coef_re, coef_im, weight, cell_count)
    right_side = jnp.concatenate(
        (jnp.concatenate((step_re, -step_im), 0), jnp.concatenate((step_im, step_re), 0)), 1
    )
    synthesis = split_einsum("ka,kp->ap", table, right_side)
    scale_back = 1.0 / math.sqrt(kept_count)
    update = jnp.stack((synthesis[:, :pixel_count], synthesis[:, pixel_count:])) * scale_back
    update = update.astype(jnp.bfloat16).reshape(2, angle_count, row_local, col_count)
    return (lax.all_to_all(update, "ang", split_axis=1, concat_axis=2, tiled=True), harmonic_rms)


def body(grads, circle_pos, harmonics, support):
    ang_count = lax.axis_size("ang")
    row_pix = grads.shape[2]
    row_local = row_pix // ang_count
    col_count = grads.shape[3]
    row_start = lax.axis_index("pix") * row_pix + lax.axis_index("ang") * row_local
    weight = (
        lax.dynamic_slice_in_dim(support, row_start, row_local, 0).astype(jnp.float32).reshape(-1)
    )
    cell_count = float(row_pix * lax.axis_size("pix") * col_count)
    update, harmonic_rms = direct_path(grads, circle_pos, harmonics, weight, cell_count)
    return (update, harmonic_rms)


def solution(mesh):
    placed = (P(None, "ang", "pix", None), P(), P(), P())
    return jax.shard_map(
        body,
        mesh=mesh,
        in_specs=placed,
        out_specs=(P(None, "ang", "pix", None), P()),
        check_vma=False,
    )
```

profile of v0, /device:TPU:1, one launch (start us, length us, event | category | flops | bytes accessed | tf_op | source)
XLA Modules:
  0.0 437.9 jit_solution(5942899219189294290)
XLA Ops:
  0.6 11.5 %copy.18 = bf16[2,64,64,512]{3,1,0,2:T(8,128)(2,1)} copy(bf16[2,64,64,512]{3,2,1,0:T(8,128)(2,1)} %param.4) | data formatting | bytes 16777216 | tf_op args[0]
  12.1 0.0 copy-start.6
  12.1 0.0 copy-start.8
  12.1 11.2 %all-to-all-start = ((bf16[2,64,64,512]{3,1,0,2:T(8,128)(2,1)}), bf16[2,64,64,512]{3,1,0,2:T(8,128)(2,1)}, u32[]{:S(2)}, u32[]{:S(2)}) async-start(bf16[2,64,64,512]{3,1,0,2:T(8,128)(2,1)} %copy.18), calls=%async_computation | async-start | bytes 16777216 | tf_op jit(solution)/shard_map/all_to_all | solution.py:44
  23.3 0.7 dynamic-slice_convert_fusion
  24.1 0.0 copy-done.6
  24.1 0.0 copy-done.8
  24.1 18.0 %fusion.8 = (f32[256,4096]{1,0:T(8,128)}, f32[256,4096]{1,0:T(8,128)}) fusion(s32[4096]{0:T(1024)S(1)} %copy-done.6, s32[256]{0:T(256)S(1)} %copy-done.8), kind=kLoop, calls=%fused_computation.23 | loop fusion | flops 14680064 | bytes 8406016 | tf_op jit(solution)/shard_map/cos | solution.py:10
  42.1 84.6 %all-to-all-done = bf16[2,64,64,512]{3,1,0,2:T(8,128)(2,1)} async-done(((bf16[2,64,64,512]{3,1,0,2:T(8,128)(2,1)}), bf16[2,64,64,512]{3,1,0,2:T(8,128)(2,1)}, u32[]{:S(2)}, u32[]{:S(2)}) %all-to-all-start) | async-done | bytes 8388640 | tf_op jit(solution)/shard_map/all_to_all | solution.py:44
  126.7 7.9 %copy.24 = bf16[2,64,64,512]{3,1,2,0:T(8,128)(2,1)} copy(bf16[2,64,64,512]{3,1,0,2:T(8,128)(2,1)} %all-to-all-done) | data formatting | bytes 16777216 | tf_op jit(solution)/shard_map/all_to_all | solution.py:44
  134.6 0.0 copy-start
  134.6 0.0 copy-start.2
  134.6 5.4 %fusion.27 = (bf16[1,64,64,1,512]{4,2,1,3,0:T(8,128)(2,1)S(1)}, bf16[1,64,64,1,512]{4,2,1,3,0:T(8,128)(2,1)}) fusion(bf16[2,64,64,1,512]{4,2,1,3,0:T(8,128)(2,1)} %bitcast.17), kind=kLoop, calls=%fused_computation.41 | loop fusion | bytes 16777216 | tf_op jit(solution)/shard_map/slice | solution.py:51
  140.0 0.0 copy-start.5
  140.0 2.1 copy-done.5
  142.1 0.0 copy-done
  142.1 1.5 copy-done.2
  143.6 8.0 %fusion.2 = f32[512,1024]{1,0:T(8,128)} fusion(bf16[4096,512]{1,0:T(8,128)(2,1)} %bitcast.21, bf16[4096,512]{1,0:T(8,128)(2,1)S(1)} %bitcast.19, f32[256,4096]{1,0:T(8,128)S(1)} %copy-done.2, f32[256,4096]{1,0:T(8,128)S(1)} %copy-done), kind=kOutput, calls=%fused_computation.15 | convolution fusion | flops 4322230272 | bytes 18874368 | tf_op jit(solution)/shard_map/ka,ap->kp/dot_general | solution.py:28
  151.6 8.5 %fusion.9 = f32[512,1024]{1,0:T(8,128)S(1)} fusion(f32[512,1024]{1,0:T(8,128)} %fusion.2, bf16[4096,512]{1,0:T(8,128)(2,1)} %bitcast.22, bf16[4096,512]{1,0:T(8,128)(2,1)} %bitcast.20, f32[256,4096]{1,0:T(8,128)S(1)} %copy-done.2, f32[256,4096]{1,0:T(8,128)S(1)} %copy-done), kind=kOutput, calls=%fused_computation.24 | convolution fusion | flops 4320657408 | bytes 20971520 | tf_op jit(solution)/shard_map/ka,ap->kp/dot_general | solution.py:28
  160.1 0.0 copy-start.4
  160.2 1.3 copy-done.4
  161.5 0.2 multiply_reduce_fusion
  161.7 70.5 %psum.7 = f32[256]{0:T(256)S(1)} all-reduce(f32[256]{0:T(256)S(1)} %multiply_reduce_fusion), channel_id=1, replica_groups=mesh['ang'=64,'pix'=2] {'ang','pix'}, use_global_device_ids=true, to_apply=%region_1.2 | all-reduce | flops 256 | bytes 2048 | tf_op jit(solution)/shard_map/psum | solution.py:35
  232.2 0.0 copy-start.7
  232.3 1.7 fusion.26
  234.0 0.0 copy-start.1
  234.0 0.0 copy-start.3
  234.0 12.7 %fusion.11 = f32[4096,1024]{1,0:T(8,128)} fusion(f32[256,512]{1,0:T(8,128)S(1)} %get-tuple-element.12, f32[256,512]{1,0:T(8,128)S(1)} %get-tuple-element.7, f32[256,512]{1,0:T(8,128)S(1)} %get-tuple-element.6, f32[256,4096]{1,0:T(8,128)} %get-tuple-element.14, f32[256,4096]{1,0:T(8,128)} %get-tuple-element.13), kind=kOutput, calls=%fused_computation.26 | convolution fusion | flops 4307025920 | bytes 26738688 | tf_op jit(solution)/shard_map/ka,kp->ap/dot_general | solution.py:28
  246.7 0.0 copy-done.7
  246.7 0.0 copy-done.1
  246.7 0.0 copy-done.3
  246.7 8.2 %fusion.19 = f32[4096,1024]{1,0:T(8,128)} fusion(f32[256,512]{1,0:T(8,128)S(1)} %get-tuple-element.12, f32[256,512]{1,0:T(8,128)S(1)} %get-tuple-element.7, f32[256,512]{1,0:T(8,128)S(1)} %get-tuple-element.6, f32[256,4096]{1,0:T(8,128)S(1)} %copy-done.3, f32[256,4096]{1,0:T(8,128)S(1)} %copy-done.1), kind=kOutput, calls=%fused_computation.39 | convolution fusion | flops 4307550208 | bytes 26738688 | tf_op jit(solution)/shard_map/ka,kp->ap/dot_general | solution.py:28
  254.9 19.3 %add_add_fusion = f32[4096,1024]{1,0:T(8,128)} fusion(f32[4096,1024]{1,0:T(8,128)} %fusion.19, f32[4096,1024]{1,0:T(8,128)} %fusion.11, f32[256,512]{1,0:T(8,128)S(1)} %get-tuple-element.12, f32[256,512]{1,0:T(8,128)S(1)} %get-tuple-element.7, f32[256,512]{1,0:T(8,128)S(1)} %get-tuple-element.6, f32[256,4096]{1,0:T(8,128)} %get-tuple-element.14, ...), kind=kOutput, calls=%fused_computation.2 | convolution fusion | flops 4318035968 | bytes 60293120 | tf_op jit(solution)/shard_map/ka,kp->ap/dot_general | solution.py:28
  274.1 6.9 %slice_bitcast_fusion.1 = (f32[1,4096,1,512]{3,1,2,0:T(8,128)S(1)}, f32[1,4096,1,512]{3,1,2,0:T(8,128)S(1)}) fusion(f32[4096,1024]{1,0:T(8,128)} %add_add_fusion), kind=kLoop, calls=%fused_computation.4 | loop fusion | bytes 33554432 | tf_op jit(solution)/shard_map/stack | solution.py:61
  281.0 2.5 fusion
  283.5 32.6 %copy.20 = bf16[2,4096,1,512]{3,0,2,1:T(2,128)(2,1)S(1)} copy(bf16[2,4096,1,512]{3,1,2,0:T(8,128)(2,1)S(1)} %fusion) | data formatting | bytes 16777216 | tf_op jit(solution)/shard_map/convert_element_type | solution.py:62
  316.2 102.3 %all_to_all.33 = bf16[2,4096,1,512]{3,0,2,1:T(2,128)(2,1)} all-to-all(bf16[2,4096,1,512]{3,0,2,1:T(2,128)(2,1)S(1)} %copy.20), channel_id=1, replica_groups=mesh['ang'=64,'pix'=2] {'ang'}, dimensions={1} | all-to-all | bytes 16777216 | tf_op jit(solution)/shard_map/all_to_all | solution.py:63
  418.4 8.0 %copy.21 = bf16[2,4096,1,512]{3,1,0,2:T(8,128)(2,1)} copy(bf16[2,4096,1,512]{3,0,2,1:T(2,128)(2,1)} %all_to_all.33) | data formatting | bytes 16777216 | tf_op jit(solution)/shard_map/all_to_all | solution.py:63
  426.4 11.5 %copy.22 = bf16[2,64,64,512]{3,2,1,0:T(8,128)(2,1)} copy(bf16[2,64,64,512]{3,1,2,0:T(8,128)(2,1)} %bitcast.18) | data formatting | bytes 16777216
  (1 shorter events, 0.0 us)
Async XLA Ops:
  12.1 11.9 %copy-start.6 = (s32[4096]{0:T(1024)S(1)}, s32[4096]{0:T(1024)}, u32[]{:S(2)}) copy-start(s32[4096]{0:T(1024)} %param.5) | copy-start | bytes 49156
  12.1 11.9 %copy-start.8 = (s32[256]{0:T(256)S(1)}, s32[256]{0:T(256)}, u32[]{:S(2)}) copy-start(s32[256]{0:T(256)} %param.6) | copy-start | bytes 3076
  12.1 114.6 %all-to-all-start = ((bf16[2,64,64,512]{3,1,0,2:T(8,128)(2,1)}), bf16[2,64,64,512]{3,1,0,2:T(8,128)(2,1)}, u32[]{:S(2)}, u32[]{:S(2)}) async-start(bf16[2,64,64,512]{3,1,0,2:T(8,128)(2,1)} %copy.18), calls=%async_computation | async-start | bytes 16777216 | tf_op jit(solution)/shard_map/all_to_all | solution.py:44
  134.6 7.5 %copy-start = (f32[256,4096]{1,0:T(8,128)S(1)}, f32[256,4096]{1,0:T(8,128)}, u32[]{:S(2)}) copy-start(f32[256,4096]{1,0:T(8,128)} %get-tuple-element.13) | copy-start | bytes 12582916
  134.6 9.0 %copy-start.2 = (f32[256,4096]{1,0:T(8,128)S(1)}, f32[256,4096]{1,0:T(8,128)}, u32[]{:S(2)}) copy-start(f32[256,4096]{1,0:T(8,128)} %get-tuple-element.14) | copy-start | bytes 12582916
  140.0 2.1 copy-start.5
  160.1 1.3 copy-start.4
  232.2 14.4 %copy-start.7 = (f32[256]{0:T(256)}, f32[256]{0:T(256)S(1)}, u32[]{:S(2)}) copy-start(f32[256]{0:T(256)S(1)} %add_sqrt_fusion) | copy-start | bytes 3076
  234.0 12.7 %copy-start.1 = (f32[256,4096]{1,0:T(8,128)S(1)}, f32[256,4096]{1,0:T(8,128)}, u32[]{:S(2)}) copy-start(f32[256,4096]{1,0:T(8,128)} %get-tuple-element.13) | copy-start | bytes 12582916
  234.0 12.7 %copy-start.3 = (f32[256,4096]{1,0:T(8,128)S(1)}, f32[256,4096]{1,0:T(8,128)}, u32[]{:S(2)}) copy-start(f32[256,4096]{1,0:T(8,128)} %get-tuple-element.14) | copy-start | bytes 12582916
where the time goes:
time: 438 us
  blocking collectives  173 us (39%)
  local copies, waits for them, and re-layouts  88.7 us (20%)
  waiting for transfers between devices  84.6 us (19%)
  matrix products  56.7 us (13%)
  other arithmetic  23.2 us (5%)
  starting transfers between devices  11.2 us (3%)
    all_to_all x1, blocking collectives, direct_path(): lax.all_to_all(update, 'ang', split_axis=1, concat_axis=2, tiled=True)  102 us
    all_to_all x1, waiting for transfers between devices, direct_path(): lax.all_to_all(grads, 'ang', split_axis=2, concat_axis=1, tiled=True)  84.6 us
    psum x1, blocking collectives, normalize(): totals = lax.psum(square_sums, ('ang', 'pix'))  70.5 us
    dot_general x5, matrix products, split_einsum(): jnp.einsum(form, left_piece, right_piece, preferred_element_type=jnp.floa...  56.7 us
    convert_element_type x1, local copies, waits for them, and re-layouts, direct_path(): update.astype(jnp.bfloat16).reshape(2, angle_count, row_local, col_count)  32.6 us
    unnamed x20, local copies, waits for them, and re-layouts  28 us
    cos x1, other arithmetic, phase_pair(): return (jnp.cos(radians), jnp.sin(radians))  18 us
    all_to_all x1, starting transfers between devices, direct_path(): lax.all_to_all(grads, 'ang', split_axis=2, concat_axis=1, tiled=True)  11.2 us
  transfers between devices with their start and end apart: 1, of which 1 were waited for; matrix products, arithmetic and copies ran while one was open for 4% of the time, Pallas kernels for 0%

commit v1 on v0

--- a/solution.py
+++ b/solution.py
@@ -32,7 +32,7 @@
 
 def normalize(coef_re, coef_im, weight, cell_count):
     square_sums = jnp.sum(weight[None, :] * (coef_re * coef_re + coef_im * coef_im), axis=1)
-    totals = lax.psum(square_sums, ("ang", "pix"))
+    totals = lax.psum(lax.psum(square_sums, "ang"), "pix")
     harmonic_rms = jnp.sqrt(totals / cell_count + 1e-06)
     factor = weight[None, :] / harmonic_rms[:, None]
     return (coef_re * factor, coef_im * factor, harmonic_rms)

time: 438 us -> 521 us (1.19)
  blocking collectives: 173 us -> 255 us
    psum x1 -> x2, blocking collectives: 70.5 us -> 148 us  [normalize(): totals = lax.psum(lax.psum(square_sums, 'ang'), 'pix')]
where the time goes in v1:
time: 521 us; the launch traced here: 520 us
  blocking collectives  255 us (49%)
  local copies, waits for them, and re-layouts  88.7 us (17%)
  waiting for transfers between devices  84.6 us (16%)
  matrix products  56.6 us (11%)
  other arithmetic  23.2 us (4%)
  starting transfers between devices  11.2 us (2%)
    psum x2, blocking collectives, normalize(): totals = lax.psum(lax.psum(square_sums, 'ang'), 'pix')  148 us
    all_to_all x1, blocking collectives, direct_path(): lax.all_to_all(update, 'ang', split_axis=1, concat_axis=2, tiled=True)  107 us
    all_to_all x1, waiting for transfers between devices, direct_path(): lax.all_to_all(grads, 'ang', split_axis=2, concat_axis=1, tiled=True)  84.6 us
    dot_general x5, matrix products, split_einsum(): jnp.einsum(form, left_piece, right_piece, preferred_element_type=jnp.floa...  56.6 us
    convert_element_type x1, local copies, waits for them, and re-layouts, direct_path(): update.astype(jnp.bfloat16).reshape(2, angle_count, row_local, col_count)  32.6 us
    unnamed x20, local copies, waits for them, and re-layouts  28 us
    cos x1, other arithmetic, phase_pair(): return (jnp.cos(radians), jnp.sin(radians))  18 us
    all_to_all x1, starting transfers between devices, direct_path(): lax.all_to_all(grads, 'ang', split_axis=2, concat_axis=1, tiled=True)  11.2 us
  transfers between devices with their start and end apart: 1, of which 1 were waited for; matrix products, arithmetic and copies ran while one was open for 4% of the time, Pallas kernels for 0%

profile of v1, /device:TPU:1, one launch (start us, length us, event | category | flops | bytes accessed | tf_op | source)
XLA Modules:
  0.0 520.3 jit_solution(9999730086849351772)
XLA Ops:
  0.6 11.5 %copy.18 = bf16[2,64,64,512]{3,1,0,2:T(8,128)(2,1)} copy(bf16[2,64,64,512]{3,2,1,0:T(8,128)(2,1)} %param.4) | data formatting | bytes 16777216 | tf_op args[0]
  12.1 0.0 copy-start.6
  12.1 0.0 copy-start.8
  12.1 11.2 %all-to-all-start = ((bf16[2,64,64,512]{3,1,0,2:T(8,128)(2,1)}), bf16[2,64,64,512]{3,1,0,2:T(8,128)(2,1)}, u32[]{:S(2)}, u32[]{:S(2)}) async-start(bf16[2,64,64,512]{3,1,0,2:T(8,128)(2,1)} %copy.18), calls=%async_computation | async-start | bytes 16777216 | tf_op jit(solution)/shard_map/all_to_all | solution.py:44
  23.3 0.7 dynamic-slice_convert_fusion
  24.1 0.0 copy-done.6
  24.1 0.0 copy-done.8
  24.1 18.0 %fusion.8 = (f32[256,4096]{1,0:T(8,128)}, f32[256,4096]{1,0:T(8,128)}) fusion(s32[4096]{0:T(1024)S(1)} %copy-done.6, s32[256]{0:T(256)S(1)} %copy-done.8), kind=kLoop, calls=%fused_computation.23 | loop fusion | flops 14680064 | bytes 8406016 | tf_op jit(solution)/shard_map/cos | solution.py:10
  42.1 84.6 %all-to-all-done = bf16[2,64,64,512]{3,1,0,2:T(8,128)(2,1)} async-done(((bf16[2,64,64,512]{3,1,0,2:T(8,128)(2,1)}), bf16[2,64,64,512]{3,1,0,2:T(8,128)(2,1)}, u32[]{:S(2)}, u32[]{:S(2)}) %all-to-all-start) | async-done | bytes 8388640 | tf_op jit(solution)/shard_map/all_to_all | solution.py:44
  126.7 7.9 %copy.24 = bf16[2,64,64,512]{3,1,2,0:T(8,128)(2,1)} copy(bf16[2,64,64,512]{3,1,0,2:T(8,128)(2,1)} %all-to-all-done) | data formatting | bytes 16777216 | tf_op jit(solution)/shard_map/all_to_all | solution.py:44
  134.6 0.0 copy-start
  134.6 0.0 copy-start.2
  134.6 5.4 %fusion.27 = (bf16[1,64,64,1,512]{4,2,1,3,0:T(8,128)(2,1)S(1)}, bf16[1,64,64,1,512]{4,2,1,3,0:T(8,128)(2,1)}) fusion(bf16[2,64,64,1,512]{4,2,1,3,0:T(8,128)(2,1)} %bitcast.17), kind=kLoop, calls=%fused_computation.41 | loop fusion | bytes 16777216 | tf_op jit(solution)/shard_map/slice | solution.py:51
  140.0 0.0 copy-start.5
  140.0 2.1 copy-done.5
  142.1 0.0 copy-done
  142.1 1.5 copy-done.2
  143.6 8.0 %fusion.2 = f32[512,1024]{1,0:T(8,128)} fusion(bf16[4096,512]{1,0:T(8,128)(2,1)} %bitcast.21, bf16[4096,512]{1,0:T(8,128)(2,1)S(1)} %bitcast.19, f32[256,4096]{1,0:T(8,128)S(1)} %copy-done.2, f32[256,4096]{1,0:T(8,128)S(1)} %copy-done), kind=kOutput, calls=%fused_computation.15 | convolution fusion | flops 4322230272 | bytes 18874368 | tf_op jit(solution)/shard_map/ka,ap->kp/dot_general | solution.py:28
  151.6 8.5 %fusion.9 = f32[512,1024]{1,0:T(8,128)S(1)} fusion(f32[512,1024]{1,0:T(8,128)} %fusion.2, bf16[4096,512]{1,0:T(8,128)(2,1)} %bitcast.22, bf16[4096,512]{1,0:T(8,128)(2,1)} %bitcast.20, f32[256,4096]{1,0:T(8,128)S(1)} %copy-done.2, f32[256,4096]{1,0:T(8,128)S(1)} %copy-done), kind=kOutput, calls=%fused_computation.24 | convolution fusion | flops 4320657408 | bytes 20971520 | tf_op jit(solution)/shard_map/ka,ap->kp/dot_general | solution.py:28
  160.1 0.0 copy-start.4
  160.2 1.3 copy-done.4
  161.5 0.2 multiply_reduce_fusion
  161.7 142.8 %psum.14 = f32[256]{0:T(256)S(1)} all-reduce(f32[256]{0:T(256)S(1)} %multiply_reduce_fusion), channel_id=1, replica_groups=mesh['ang'=64,'pix'=2] {'ang'}, use_global_device_ids=true, to_apply=%region_1.2 | all-reduce | flops 256 | bytes 2048 | tf_op jit(solution)/shard_map/psum | solution.py:35
  304.5 5.5 %psum.15 = f32[256]{0:T(256)S(1)} all-reduce(f32[256]{0:T(256)S(1)} %psum.14), channel_id=1, replica_groups=mesh['ang'=64,'pix'=2] {'pix'}, use_global_device_ids=true, to_apply=%region_2.3 | all-reduce | flops 256 | bytes 2048 | tf_op jit(solution)/shard_map/psum | solution.py:35
  310.0 0.0 copy-start.7
  310.0 1.7 fusion.26
  311.8 0.0 copy-start.1
  311.8 0.0 copy-start.3
  311.8 12.6 %fusion.11 = f32[4096,1024]{1,0:T(8,128)} fusion(f32[256,512]{1,0:T(8,128)S(1)} %get-tuple-element.12, f32[256,512]{1,0:T(8,128)S(1)} %get-tuple-element.7, f32[256,512]{1,0:T(8,128)S(1)} %get-tuple-element.6, f32[256,4096]{1,0:T(8,128)} %get-tuple-element.14, f32[256,4096]{1,0:T(8,128)} %get-tuple-element.13), kind=kOutput, calls=%fused_computation.26 | convolution fusion | flops 4307025920 | bytes 26738688 | tf_op jit(solution)/shard_map/ka,kp->ap/dot_general | solution.py:28
  324.4 0.0 copy-done.7
  324.4 0.0 copy-done.1
  324.4 0.0 copy-done.3
  324.4 8.2 %fusion.19 = f32[4096,1024]{1,0:T(8,128)} fusion(f32[256,512]{1,0:T(8,128)S(1)} %get-tuple-element.12, f32[256,512]{1,0:T(8,128)S(1)} %get-tuple-element.7, f32[256,512]{1,0:T(8,128)S(1)} %get-tuple-element.6, f32[256,4096]{1,0:T(8,128)S(1)} %copy-done.3, f32[256,4096]{1,0:T(8,128)S(1)} %copy-done.1), kind=kOutput, calls=%fused_computation.39 | convolution fusion | flops 4307550208 | bytes 26738688 | tf_op jit(solution)/shard_map/ka,kp->ap/dot_general | solution.py:28
  332.6 19.2 %add_add_fusion = f32[4096,1024]{1,0:T(8,128)} fusion(f32[4096,1024]{1,0:T(8,128)} %fusion.19, f32[4096,1024]{1,0:T(8,128)} %fusion.11, f32[256,512]{1,0:T(8,128)S(1)} %get-tuple-element.12, f32[256,512]{1,0:T(8,128)S(1)} %get-tuple-element.7, f32[256,512]{1,0:T(8,128)S(1)} %get-tuple-element.6, f32[256,4096]{1,0:T(8,128)} %get-tuple-element.14, ...), kind=kOutput, calls=%fused_computation.2 | convolution fusion | flops 4318035968 | bytes 60293120 | tf_op jit(solution)/shard_map/ka,kp->ap/dot_general | solution.py:28
  351.8 6.9 %slice_bitcast_fusion.1 = (f32[1,4096,1,512]{3,1,2,0:T(8,128)S(1)}, f32[1,4096,1,512]{3,1,2,0:T(8,128)S(1)}) fusion(f32[4096,1024]{1,0:T(8,128)} %add_add_fusion), kind=kLoop, calls=%fused_computation.4 | loop fusion | bytes 33554432 | tf_op jit(solution)/shard_map/stack | solution.py:61
  358.7 2.5 fusion
  361.2 32.6 %copy.20 = bf16[2,4096,1,512]{3,0,2,1:T(2,128)(2,1)S(1)} copy(bf16[2,4096,1,512]{3,1,2,0:T(8,128)(2,1)S(1)} %fusion) | data formatting | bytes 16777216 | tf_op jit(solution)/shard_map/convert_element_type | solution.py:62
  393.8 107.0 %all_to_all.33 = bf16[2,4096,1,512]{3,0,2,1:T(2,128)(2,1)} all-to-all(bf16[2,4096,1,512]{3,0,2,1:T(2,128)(2,1)S(1)} %copy.20), channel_id=1, replica_groups=mesh['ang'=64,'pix'=2] {'ang'}, dimensions={1} | all-to-all | bytes 16777216 | tf_op jit(solution)/shard_map/all_to_all | solution.py:63
  500.8 8.0 %copy.21 = bf16[2,4096,1,512]{3,1,0,2:T(8,128)(2,1)} copy(bf16[2,4096,1,512]{3,0,2,1:T(2,128)(2,1)} %all_to_all.33) | data formatting | bytes 16777216 | tf_op jit(solution)/shard_map/all_to_all | solution.py:63
  508.7 11.5 %copy.22 = bf16[2,64,64,512]{3,2,1,0:T(8,128)(2,1)} copy(bf16[2,64,64,512]{3,1,2,0:T(8,128)(2,1)} %bitcast.18) | data formatting | bytes 16777216
  (1 shorter events, 0.0 us)
Async XLA Ops:
  12.1 11.9 %copy-start.6 = (s32[4096]{0:T(1024)S(1)}, s32[4096]{0:T(1024)}, u32[]{:S(2)}) copy-start(s32[4096]{0:T(1024)} %param.5) | copy-start | bytes 49156
  12.1 11.9 %copy-start.8 = (s32[256]{0:T(256)S(1)}, s32[256]{0:T(256)}, u32[]{:S(2)}) copy-start(s32[256]{0:T(256)} %param.6) | copy-start | bytes 3076
  12.1 114.6 %all-to-all-start = ((bf16[2,64,64,512]{3,1,0,2:T(8,128)(2,1)}), bf16[2,64,64,512]{3,1,0,2:T(8,128)(2,1)}, u32[]{:S(2)}, u32[]{:S(2)}) async-start(bf16[2,64,64,512]{3,1,0,2:T(8,128)(2,1)} %copy.18), calls=%async_computation | async-start | bytes 16777216 | tf_op jit(solution)/shard_map/all_to_all | solution.py:44
  134.6 7.5 %copy-start = (f32[256,4096]{1,0:T(8,128)S(1)}, f32[256,4096]{1,0:T(8,128)}, u32[]{:S(2)}) copy-start(f32[256,4096]{1,0:T(8,128)} %get-tuple-element.13) | copy-start | bytes 12582916
  134.6 9.0 %copy-start.2 = (f32[256,4096]{1,0:T(8,128)S(1)}, f32[256,4096]{1,0:T(8,128)}, u32[]{:S(2)}) copy-start(f32[256,4096]{1,0:T(8,128)} %get-tuple-element.14) | copy-start | bytes 12582916
  140.0 2.1 copy-start.5
  160.1 1.3 copy-start.4
  310.0 14.4 %copy-start.7 = (f32[256]{0:T(256)}, f32[256]{0:T(256)S(1)}, u32[]{:S(2)}) copy-start(f32[256]{0:T(256)S(1)} %add_sqrt_fusion) | copy-start | bytes 3076
  311.8 12.7 %copy-start.1 = (f32[256,4096]{1,0:T(8,128)S(1)}, f32[256,4096]{1,0:T(8,128)}, u32[]{:S(2)}) copy-start(f32[256,4096]{1,0:T(8,128)} %get-tuple-element.13) | copy-start | bytes 12582916
  311.8 12.7 %copy-start.3 = (f32[256,4096]{1,0:T(8,128)S(1)}, f32[256,4096]{1,0:T(8,128)}, u32[]{:S(2)}) copy-start(f32[256,4096]{1,0:T(8,128)} %get-tuple-element.14) | copy-start | bytes 12582916
